TPU v7x, 32 devices: a whole 2x2x4 slice. The times are simulated.
32 devices in a mesh: groups: 2 (over x), tensor: 16 (over z, y, core).
Axes of the slice: x: 2, y: 2, z: 4, core: 2. Of those that a mesh axis runs over, the one named last changes fastest.
Arguments:
- tokens: bfloat16 [256, 8192], P(('groups', 'tensor')), parts along dimension 0, may hold values from -6 to 6
- gate_weight: bfloat16 [8192, 28672], P(None, 'tensor'), may hold values from -0.0625 to 0.0625
- up_weight: bfloat16 [8192, 28672], P(None, 'tensor'), may hold values from -0.0625 to 0.0625
- adapter_down_weight: bfloat16 [16, 8192, 64], P('tensor'), may hold values from -0.0625 to 0.0625
- adapter_up_weight: bfloat16 [16, 64, 28672], P(None, None, 'tensor'), may hold values from -0.75 to 0.75
- token_adapter_index: int32 [256, 1], P(('groups', 'tensor')), parts along dimension 0, may hold values from 0 to 15; in each aligned block of 128 rows (0 to 127, 128 to 255, ...) at most 16 rows name the same one
- adapter_slot_index: int32 [16], replicated, may hold values from 0 to 15, each once
Outputs:
- hidden: bfloat16 [256, 28672], P('groups', 'tensor'), parts along dimension 0
There are 2 independent parts, one for each index of `groups`. A program takes and returns all parts, laid end to end along the dimension named above; an argument that names none is the same for every part. Nothing has to cross between parts.
Inputs may be any that keep to these rules, and one draw needn't show every extreme that they name: `token_adapter_index`: in every draw at most 16 of all 128 tokens use one adapter, and some adapter is used by exactly 16 tokens; every adapter is used by some token. `adapter_slot_index`: A permutation; slot s is stored on the device of index s along tensor.
All inputs are finite; a program needn't handle non-finite values.
Results may differ from a plain program's by a relative error of at most 0.0039.
Values may be sent and summed in bfloat16 or wider, within the bound.
No kernel may reach another device: no remote copies, remote signals or barrier semaphores. Data moves between devices by JAX's collectives and lax.ppermute only.
A program may use at most 192 MiB of HBM per device.

v0:
```python
import jax
import jax.numpy as jnp
from jax import lax
from jax.sharding import PartitionSpec as P

CHUNKS = 2
LANES = 128


def body(
    tokens,
    gate_weight,
    up_weight,
    adapter_down_weight,
    adapter_up_weight,
    token_adapter_index,
    adapter_slot_index,
):
    me = lax.axis_index("tensor")
    rows, width = tokens.shape
    step = width // CHUNKS
    local_slot = jnp.take(adapter_slot_index, token_adapter_index[:, 0], axis=0)
    slot_cols = jnp.broadcast_to(local_slot.astype(jnp.bfloat16)[:, None], (rows, LANES))
    gate = up = low = None
    slots = None
    for c in range(CHUNKS):
        piece = tokens[:, c * step : (c + 1) * step]
        if c == CHUNKS - 1:
            piece = jnp.concatenate([piece, slot_cols], axis=1)
        gathered = lax.all_gather(piece, "tensor", axis=0, tiled=True)
        if c == CHUNKS - 1:
            slots = gathered[:, step].astype(jnp.int32)
            gathered = gathered[:, :step]
        g = jnp.dot(
            gathered, gate_weight[c * step : (c + 1) * step], preferred_element_type=jnp.float32
        )
        u = jnp.dot(
            gathered, up_weight[c * step : (c + 1) * step], preferred_element_type=jnp.float32
        )
        d = jnp.dot(
            gathered,
            adapter_down_weight[0, c * step : (c + 1) * step],
            preferred_element_type=jnp.float32,
        )
        gate = g if gate is None else gate + g
        up = u if up is None else up + u
        low = d if low is None else low + d
    mine = slots == me
    low = jnp.where(mine[:, None], low, 0.0).astype(jnp.bfloat16)
    spread = lax.all_gather(low, "tensor", axis=0, tiled=False)
    delta = jnp.einsum("str,srh->th", spread, adapter_up_weight, preferred_element_type=jnp.float32)
    return (jax.nn.silu(gate) * (up + delta)).astype(jnp.bfloat16)


def solution(mesh):
    in_specs = (
        P(("groups", "tensor"), None),
        P(None, "tensor"),
        P(None, "tensor"),
        P("tensor", None, None),
        P(None, None, "tensor"),
        P(("groups", "tensor"), None),
        P(),
    )
    out_specs = P("groups", "tensor")
    return jax.shard_map(body, mesh=mesh, in_specs=in_specs, out_specs=out_specs, check_vma=False)
```

profile of v0, /device:TPU:0, one launch (start us, length us, event | category | flops | bytes accessed | tf_op | source)
XLA Modules:
  0.0 148.9 jit_solution(2792847004383480132)
XLA Ops:
  6.5 0.0 copy-start
  6.5 0.0 all-gather.4.cloned.1.call-start
  6.5 1.5 %fusion.40 = (bf16[8,4096]{1,0:T(8,128)(2,1)}, bf16[8,4096]{1,0:T(8,128)(2,1)S(1)}) fusion(bf16[8,8192]{1,0:T(8,128)(2,1)} %param.7), kind=kLoop, calls=%fused_computation.36 | loop fusion | bytes 262144 | tf_op jit(solution)/shard_map/slice | solution.py:27
  8.0 0.0 all-gather.4.cloned.1.call-update
  8.1 0.0 all-gather.6.cloned.1.call-start
  8.1 0.7 fusion.39
  8.8 0.0 copy-done
  8.8 0.6 gather_fusion
  9.4 0.7 convert_bitcast_fusion
  10.1 0.1 broadcast_in_dim.26
  10.2 0.6 pad_maximum_fusion
  10.8 0.0 all-gather.6.cloned.1.call-update
  10.8 39.3 %all-gather.4.cloned.1.call-done = bf16[128,4096]{1,0:T(8,128)(2,1)} async-done(((bf16[8,4096]{1,0:T(8,128)(2,1)}), bf16[128,4096]{1,0:T(8,128)(2,1)}) %all-gather.4.cloned.1.call-update) | async-done | bytes 1048592 | tf_op jit(solution)/shard_map/all_gather | solution.py:30
  50.2 1.8 %fusion.34 = f32[128,64]{0,1:T(8,128)S(1)} fusion(bf16[128,4096]{1,0:T(8,128)(2,1)} %all-gather.4.cloned.1.call-done, bf16[1,8192,64]{1,2,0:T(8,128)(2,1)} %param.10), kind=kOutput, calls=%fused_computation.24 | convolution fusion | flops 67108864 | bytes 1605632 | tf_op jit(solution)/shard_map/dot_general | solution.py:40
  52.0 37.4 %all-gather.6.cloned.1.call-done = bf16[128,4224]{1,0:T(8,128)(2,1)} async-done(((bf16[8,4224]{1,0:T(8,128)(2,1)}), bf16[128,4224]{1,0:T(8,128)(2,1)}) %all-gather.6.cloned.1.call-update) | async-done | bytes 1081360 | tf_op jit(solution)/shard_map/all_gather | solution.py:30
  89.4 0.0 copy-start.3
  89.4 1.0 fusion.38
  90.4 1.8 %fusion.29 = bf16[128,64]{0,1:T(8,128)(2,1)S(1)} fusion(f32[128,64]{0,1:T(8,128)S(1)} %fusion.34, bf16[128,4224]{1,0:T(8,128)(2,1)} %all-gather.6.cloned.1.call-done, bf16[1,8192,64]{1,2,0:T(8,128)(2,1)} %param.10, pred[128]{0:T(512)(128)(4,1)S(1)} %fusion.38), kind=kOutput, calls=%fused_computation.19 | convolution fusion | flops 67133440 | bytes 1622144 | tf_op jit(solution)/shard_map/dot_general | solution.py:40
  92.2 20.1 %all-gather = bf16[2048,64]{0,1:T(8,128)(2,1)S(1)} all-gather(bf16[128,64]{0,1:T(8,128)(2,1)S(1)} %fusion.29), channel_id=2, replica_groups=mesh['groups'=2,'tensor'=16] {'tensor'}, dimensions={0}, use_global_device_ids=true | all-gather | bytes 278528 | tf_op jit(solution)/shard_map/all_gather | solution.py:50
  112.4 6.8 %fusion = f32[128,1792]{1,0:T(8,128)S(1)} fusion(bf16[8192,1792]{1,0:T(8,128)(2,1)} %param.9, bf16[128,4224]{1,0:T(8,128)(2,1)} %all-gather.6.cloned.1.call-done), kind=kOutput, calls=%fused_computation.1 | convolution fusion | flops 1879048192 | bytes 16646144 | tf_op jit(solution)/shard_map/dot_general | solution.py:37
  119.2 0.0 copy-done.3
  119.2 0.0 copy-start.2
  119.2 6.5 %fusion.4 = f32[128,1792]{1,0:T(8,128)S(1)} fusion(bf16[8192,1792]{1,0:T(8,128)(2,1)} %param.8, bf16[128,4224]{1,0:T(8,128)(2,1)S(1)} %copy-done.3), kind=kOutput, calls=%fused_computation.5 | convolution fusion | flops 1879048192 | bytes 16646144 | tf_op jit(solution)/shard_map/dot_general | solution.py:34
  125.7 0.0 copy-done.2
  125.7 6.5 %fusion.13 = f32[128,1792]{1,0:T(8,128)S(1)} fusion(f32[128,1792]{1,0:T(8,128)S(1)} %fusion.4, bf16[128,4096]{1,0:T(8,128)(2,1)S(1)} %copy-done.2, bf16[8192,1792]{1,0:T(8,128)(2,1)} %param.8), kind=kOutput, calls=%fused_computation.12 | convolution fusion | flops 1879277568 | bytes 17563648 | tf_op jit(solution)/shard_map/dot_general | solution.py:34
  132.2 0.0 copy-start.4
  132.2 0.0 copy-start.1
  132.2 6.6 %fusion.16 = f32[128,1792]{1,0:T(8,128)S(1)} fusion(f32[128,1792]{1,0:T(8,128)S(1)} %fusion, bf16[128,4096]{1,0:T(8,128)(2,1)S(1)} %copy-done.2, bf16[8192,1792]{1,0:T(8,128)(2,1)} %param.9), kind=kOutput, calls=%fused_computation.13 | convolution fusion | flops 1879277568 | bytes 17563648 | tf_op jit(solution)/shard_map/dot_general | solution.py:37
  138.9 0.0 copy-done.4
  138.9 3.2 %fusion.25 = bf16[128,1792]{1,0:T(8,128)(2,1)} fusion(f32[128,1792]{1,0:T(8,128)S(1)} %fusion.16, bf16[16,128,64]{1,0,2:T(8,128)(2,1)S(1)} %bitcast.31, bf16[16,64,1792]{2,1,0:T(8,128)(2,1)S(1)} %copy-done.4, f32[128,1792]{1,0:T(8,128)S(1)} %fusion.13), kind=kOutput, calls=%fused_computation.16 | convolution fusion | flops 471367680 | bytes 6225920 | tf_op jit(solution)/shard_map/str,srh->th/dot_general | solution.py:51
  142.1 0.0 copy-done.1
  (2 shorter events, 0.0 us)
Async XLA Ops:
  6.5 2.3 %copy-start = (s32[16]{0:T(128)S(1)}, s32[16]{0:T(128)}, u32[]{:S(2)}) copy-start(s32[16]{0:T(128)} %param.13) | copy-start | bytes 196
  6.5 43.7 %all-gather.4.cloned.1.call-start = ((), (), s32[]{:S(2)}) async-start(), calls=%async_computation | async-start | bytes 1114112 | tf_op jit(solution)/shard_map/all_gather | solution.py:30
  8.1 81.3 %all-gather.6.cloned.1.call-start = ((), (), s32[]{:S(2)}) async-start(), calls=%async_computation.1 | async-start | bytes 1148928 | tf_op jit(solution)/shard_map/all_gather | solution.py:30
  89.4 29.8 %copy-start.3 = (bf16[128,4224]{1,0:T(8,128)(2,1)S(1)}, bf16[128,4224]{1,0:T(8,128)(2,1)}, u32[]{:S(2)}) copy-start(bf16[128,4224]{1,0:T(8,128)(2,1)} %all-gather.6.cloned.1.call-done) | copy-start | bytes 3244036
  119.2 6.6 %copy-start.2 = (bf16[128,4096]{1,0:T(8,128)(2,1)S(1)}, bf16[128,4096]{1,0:T(8,128)(2,1)}, u32[]{:S(2)}) copy-start(bf16[128,4096]{1,0:T(8,128)(2,1)} %all-gather.4.cloned.1.call-done) | copy-start | bytes 3145732
  132.2 6.7 %copy-start.4 = (bf16[16,64,1792]{2,1,0:T(8,128)(2,1)S(1)}, bf16[16,64,1792]{2,1,0:T(8,128)(2,1)}, u32[]{:S(2)}) copy-start(bf16[16,64,1792]{2,1,0:T(8,128)(2,1)} %param.11) | copy-start | bytes 11010052
  132.2 9.8 %copy-start.1 = (s32[16]{0:T(128)S(1)}, s32[16]{0:T(128)}, u32[]{:S(2)}) copy-start(s32[16]{0:T(128)} %param.13) | copy-start | bytes 196
Sparse Core Ops, SparseCore 0:
  9.5 40.6 all-gather.3
  52.4 36.9 all-gather.5
where the time goes:
time: 149 us
  waiting for transfers between devices  76.7 us (51%)
  matrix products  33.3 us (22%)
  blocking collectives  20.1 us (13%)
  between operations  13.5 us (9%)
  other arithmetic  2.93 us (2%)
  local copies, waits for them, and re-layouts  2.29 us (2%)
    all_gather x2, waiting for transfers between devices, body(): gathered = lax.all_gather(piece, 'tensor', axis=0, tiled=True)  76.7 us
    all_gather x1, blocking collectives, body(): spread = lax.all_gather(low, 'tensor', axis=0, tiled=False)  20.1 us
    dot_general x2, matrix products, body(): jnp.dot(gathered, up_weight[c * step:(c + 1) * step], preferred_element_t...  13.4 us
    dot_general x2, matrix products, body(): jnp.dot(gathered, gate_weight[c * step:(c + 1) * step], preferred_element...  13 us
    dot_general x2, matrix products, body(): jnp.dot(gathered, adapter_down_weight[0, c * step:(c + 1) * step], prefer...  3.68 us
    dot_general x1, matrix products, body(): jnp.einsum('str,srh->th', spread, adapter_up_weight, preferred_element_ty...  3.19 us
  transfers between devices with their start and end apart: 2, of which 2 were waited for; matrix products, arithmetic and copies ran while one was open for 3% of the time, Pallas kernels for 0%

commit v1 on v0

--- a/solution.py
+++ b/solution.py
@@ -5,6 +5,18 @@
 
 CHUNKS = 2
 LANES = 128
+
+
+def gather_by_bits(x, axis, dim):
+    ways, here = (lax.axis_size(axis), lax.axis_index(axis))
+    grown, reach = (x, 1)
+    while reach < ways:
+        theirs = lax.ppermute(grown, axis, [(d, d ^ reach) for d in range(ways)])
+        mine_first = jnp.concatenate([grown, theirs], axis=dim)
+        theirs_first = jnp.concatenate([theirs, grown], axis=dim)
+        grown = jnp.where(here & reach == 0, mine_first, theirs_first)
+        reach = 2 * reach
+    return grown
 
 
 def body(
@@ -27,7 +39,7 @@
         piece = tokens[:, c * step : (c + 1) * step]
         if c == CHUNKS - 1:
             piece = jnp.concatenate([piece, slot_cols], axis=1)
-        gathered = lax.all_gather(piece, "tensor", axis=0, tiled=True)
+        gathered = gather_by_bits(piece, "tensor", 0)
         if c == CHUNKS - 1:
             slots = gathered[:, step].astype(jnp.int32)
             gathered = gathered[:, :step]

time: 149 us -> 119 us (0.80)
  waiting for transfers between devices: 76.7 us -> 53.9 us
  between operations: 13.5 us -> 0.15 us
  starting transfers between devices: 0.04 us -> 8.87 us
  matrix products: 33.3 us -> 30.3 us
  blocking collectives: 20.1 us -> 21.7 us
    all_gather x2 -> x0, waiting for transfers between devices: 76.7 us -> none  [body(): gathered = lax.all_gather(piece, 'tensor', axis=0, tiled=True)]
    ppermute x0 -> x8, waiting for transfers between devices: none -> 53.9 us  [gather_by_bits(): theirs = lax.ppermute(grown, axis, [(d, d ^ reach) for d in range(ways)])]
    ppermute x0 -> x8, starting transfers between devices: none -> 8.87 us  [gather_by_bits(): theirs = lax.ppermute(grown, axis, [(d, d ^ reach) for d in range(ways)])]
    dot_general x2, matrix products: 3.68 us -> 0.99 us  [body(): jnp.dot(gathered, adapter_down_weight[0, c * step:(c + 1) * step], prefer...]
    all_gather x1, blocking collectives: 20.1 us -> 21.7 us  [body(): spread = lax.all_gather(low, 'tensor', axis=0, tiled=False)]
  transfers between devices with their start and end apart: 2 -> 8, of which waited for: 2 -> 7; matrix products, arithmetic and copies ran while one was open for 3% -> 1% of each run, Pallas kernels for 0% -> 0%
where the time goes in v1:
time: 119 us
  waiting for transfers between devices  53.9 us (45%)
  matrix products  30.3 us (25%)
  blocking collectives  21.7 us (18%)
  starting transfers between devices  8.87 us (7%)
  other arithmetic  1.97 us (2%)
  local copies, waits for them, and re-layouts  1.66 us (1%)
    ppermute x8, waiting for transfers between devices, gather_by_bits(): theirs = lax.ppermute(grown, axis, [(d, d ^ reach) for d in range(ways)])  53.9 us
    all_gather x1, blocking collectives, body(): spread = lax.all_gather(low, 'tensor', axis=0, tiled=False)  21.7 us
    dot_general x2, matrix products, body(): jnp.dot(gathered, up_weight[c * step:(c + 1) * step], preferred_element_t...  13.9 us
    dot_general x2, matrix products, body(): jnp.dot(gathered, gate_weight[c * step:(c + 1) * step], preferred_element...  13.1 us
    ppermute x8, starting transfers between devices, gather_by_bits(): theirs = lax.ppermute(grown, axis, [(d, d ^ reach) for d in range(ways)])  8.87 us
  transfers between devices with their start and end apart: 8, of which 7 were waited for; matrix products, arithmetic and copies ran while one was open for 1% of the time, Pallas kernels for 0%

profile of v1, /device:TPU:0, one launch (start us, length us, event | category | flops | bytes accessed | tf_op | source)
XLA Modules:
  0.0 118.5 jit_solution(3599388652628064634)
XLA Ops:
  0.0 0.0 copy-start
  0.0 0.7 fusion.33
  0.7 0.0 copy-done
  0.7 0.6 gather_fusion
  1.3 0.7 convert_bitcast_fusion
  2.0 0.9 fusion.36
  2.9 0.1 broadcast_in_dim.26
  3.0 0.5 collective-permute-start.4
  3.4 0.1 collective-permute-start
  3.5 0.8 collective-permute-done.4
  4.4 2.9 %collective-permute-start.5 = (bf16[16,4224]{1,0:T(8,128)(2,1)S(1)}, bf16[16,4224]{1,0:T(8,128)(2,1)S(1)}, u32[]{:S(2)}, u32[]{:S(2)}) collective-permute-start(bf16[16,4224]{1,0:T(8,128)(2,1)S(1)} %maximum_select_fusion.6), channel_id=1, source_target_pairs={{0,2},{1,3},{2,0},{3,1},{4,6},{5,7},{6,4},{7,5},{8,10},{9,11},{10,... | collective-permute-start | bytes 405512 | tf_op jit(solution)/shard_map/ppermute | solution.py:14
  7.3 0.0 collective-permute-done
  7.3 0.1 collective-permute-start.1
  7.5 4.2 %collective-permute-done.5 = bf16[16,4224]{1,0:T(8,128)(2,1)S(1)} collective-permute-done((bf16[16,4224]{1,0:T(8,128)(2,1)S(1)}, bf16[16,4224]{1,0:T(8,128)(2,1)S(1)}, u32[]{:S(2)}, u32[]{:S(2)}) %collective-permute-start.5) | collective-permute-done | bytes 135200 | tf_op jit(solution)/shard_map/ppermute | solution.py:14
  11.7 2.2 %collective-permute-start.6 = (bf16[32,4224]{1,0:T(8,128)(2,1)S(1)}, bf16[32,4224]{1,0:T(8,128)(2,1)S(1)}, u32[]{:S(2)}, u32[]{:S(2)}) collective-permute-start(bf16[32,4224]{1,0:T(8,128)(2,1)S(1)} %maximum_select_fusion.4), channel_id=1, source_target_pairs={{0,4},{1,5},{2,6},{3,7},{4,0},{5,1},{6,2},{7,3},{8,12},{9,13},{10,... | collective-permute-start | bytes 811016 | tf_op jit(solution)/shard_map/ppermute | solution.py:14
  13.9 0.1 collective-permute-done.1
  14.1 0.0 copy-start.3
  14.1 1.9 %collective-permute-start.2 = (bf16[32,4096]{1,0:T(8,128)(2,1)S(1)}, bf16[32,4096]{1,0:T(8,128)(2,1)S(1)}, u32[]{:S(2)}, u32[]{:S(2)}) collective-permute-start(bf16[32,4096]{1,0:T(8,128)(2,1)S(1)} %maximum_select_fusion.5), channel_id=1, source_target_pairs={{0,4},{1,5},{2,6},{3,7},{4,0},{5,1},{6,2},{7,3},{8,12},{9,13},{10,... | collective-permute-start | bytes 786440 | tf_op jit(solution)/shard_map/ppermute | solution.py:14
  15.9 8.7 %collective-permute-done.6 = bf16[32,4224]{1,0:T(8,128)(2,1)S(1)} collective-permute-done((bf16[32,4224]{1,0:T(8,128)(2,1)S(1)}, bf16[32,4224]{1,0:T(8,128)(2,1)S(1)}, u32[]{:S(2)}, u32[]{:S(2)}) %collective-permute-start.6) | collective-permute-done | bytes 270368 | tf_op jit(solution)/shard_map/ppermute | solution.py:14
  24.6 0.1 maximum_select_fusion.2
  24.7 1.2 collective-permute-start.7
  25.9 4.9 %collective-permute-done.2 = bf16[32,4096]{1,0:T(8,128)(2,1)S(1)} collective-permute-done((bf16[32,4096]{1,0:T(8,128)(2,1)S(1)}, bf16[32,4096]{1,0:T(8,128)(2,1)S(1)}, u32[]{:S(2)}, u32[]{:S(2)}) %collective-permute-start.2) | collective-permute-done | bytes 262176 | tf_op jit(solution)/shard_map/ppermute | solution.py:14
  30.8 0.1 maximum_select_fusion.3
  30.9 0.1 collective-permute-start.3
  30.9 30.3 %collective-permute-done.7 = bf16[64,4224]{1,0:T(8,128)(2,1)S(1)} collective-permute-done((bf16[64,4224]{1,0:T(8,128)(2,1)S(1)}, bf16[64,4224]{1,0:T(8,128)(2,1)S(1)}, u32[]{:S(2)}, u32[]{:S(2)}) %collective-permute-start.7) | collective-permute-done | bytes 540704 | tf_op jit(solution)/shard_map/ppermute | solution.py:14
  61.2 0.2 maximum_select_fusion
  61.4 0.1 fusion.32
  61.5 0.0 copy-done.3
  61.5 0.5 fusion.24
  62.0 4.8 %collective-permute-done.3 = bf16[64,4096]{1,0:T(8,128)(2,1)S(1)} collective-permute-done((bf16[64,4096]{1,0:T(8,128)(2,1)S(1)}, bf16[64,4096]{1,0:T(8,128)(2,1)S(1)}, u32[]{:S(2)}, u32[]{:S(2)}) %collective-permute-start.3) | collective-permute-done | bytes 524320 | tf_op jit(solution)/shard_map/ppermute | solution.py:14
  66.9 0.5 fusion.23
  67.4 21.7 %all-gather = bf16[2048,64]{0,1:T(8,128)(2,1)S(1)} all-gather(bf16[128,64]{0,1:T(8,128)(2,1)S(1)} %fusion.23), channel_id=2, replica_groups=mesh['groups'=2,'tensor'=16] {'tensor'}, dimensions={0}, use_global_device_ids=true | all-gather | bytes 278528 | tf_op jit(solution)/shard_map/all_gather | solution.py:62
  89.1 6.5 %fusion = f32[128,1792]{1,0:T(8,128)S(1)} fusion(bf16[8192,1792]{1,0:T(8,128)(2,1)} %param.9, bf16[128,4224]{1,0:T(8,128)(2,1)S(1)} %maximum_select_fusion), kind=kOutput, calls=%fused_computation.1 | convolution fusion | flops 1879048192 | bytes 16646144 | tf_op jit(solution)/shard_map/dot_general | solution.py:49
  95.6 0.0 copy-start.2
  95.6 6.6 %fusion.4 = f32[128,1792]{1,0:T(8,128)S(1)} fusion(bf16[8192,1792]{1,0:T(8,128)(2,1)} %param.8, bf16[128,4224]{1,0:T(8,128)(2,1)S(1)} %maximum_select_fusion), kind=kOutput, calls=%fused_computation.5 | convolution fusion | flops 1879048192 | bytes 16646144 | tf_op jit(solution)/shard_map/dot_general | solution.py:46
  102.2 0.0 copy-done.2
  102.2 2.3 %fusion.10 = f32[128,1792]{1,0:T(8,128)S(1)} fusion(bf16[16,128,64]{1,0,2:T(8,128)(2,1)S(1)} %bitcast.21, bf16[16,64,1792]{2,1,0:T(8,128)(2,1)S(1)} %copy-done.2), kind=kOutput, calls=%fused_computation.11 | convolution fusion | flops 469762048 | bytes 4849664 | tf_op jit(solution)/shard_map/str,srh->th/dot_general | solution.py:63
  104.6 6.5 %fusion.13 = f32[128,1792]{1,0:T(8,128)S(1)} fusion(f32[128,1792]{1,0:T(8,128)S(1)} %fusion.4, bf16[8192,1792]{1,0:T(8,128)(2,1)} %param.8, bf16[64,4096]{1,0:T(8,128)(2,1)S(1)} %collective-permute-done.3, bf16[64,4096]{1,0:T(8,128)(2,1)S(1)} %maximum_select_fusion.3, pred[]{:T(512)S(6)} %eq.23), kind=kOutput, calls=%fused_computation.12 | convolution fusion | flops 1883996160 | bytes 17563648 | tf_op jit(solution)/shard_map/dot_general | solution.py:46
  111.1 0.0 copy-start.1
  111.1 7.4 %multiply_convert_fusion = bf16[128,1792]{1,0:T(8,128)(2,1)} fusion(f32[128,1792]{1,0:T(8,128)S(1)} %fusion.13, f32[128,1792]{1,0:T(8,128)S(1)} %fusion.10, f32[128,1792]{1,0:T(8,128)S(1)} %fusion, bf16[8192,1792]{1,0:T(8,128)(2,1)} %param.9, bf16[64,4096]{1,0:T(8,128)(2,1)S(1)} %collective-permute-done.3, bf16[64,4096]{1,0:T(8,128)(2,1)S(1)} %maximum_select_fusion.3, ...), kind=kOutput, calls=%fused_computation.20 | convolution fusion | flops 1885601792 | bytes 18939904 | tf_op jit(solution)/shard_map/dot_general | solution.py:49
  118.5 0.0 copy-done.1
  (7 shorter events, 0.2 us)
Async XLA Ops:
  0.0 0.7 copy-start
  3.0 1.4 %collective-permute-start.4 = (bf16[8,4224]{1,0:T(8,128)(2,1)S(1)}, bf16[8,4224]{1,0:T(8,128)(2,1)S(1)}, u32[]{:S(2)}, u32[]{:S(2)}) collective-permute-start(bf16[8,4224]{1,0:T(8,128)(2,1)S(1)} %pad_maximum_fusion), channel_id=1, source_target_pairs={{0,1},{1,0},{2,3},{3,2},{4,5},{5,4},{6,7},{7,6},{8,9},{9,8},{10,11... | collective-permute-start | bytes 202760 | tf_op jit(solution)/shard_map/ppermute | solution.py:14
  3.4 3.9 %collective-permute-start = (bf16[8,4096]{1,0:T(8,128)(2,1)S(1)}, bf16[8,4096]{1,0:T(8,128)(2,1)S(1)}, u32[]{:S(2)}, u32[]{:S(2)}) collective-permute-start(bf16[8,4096]{1,0:T(8,128)(2,1)S(1)} %get-tuple-element.5), channel_id=1, source_target_pairs={{0,1},{1,0},{2,3},{3,2},{4,5},{5,4},{6,7},{7,6},{8,9},{9,8},{10,11... | collective-permute-start | bytes 196616 | tf_op jit(solution)/shard_map/ppermute | solution.py:14
  4.4 7.3 %collective-permute-start.5 = (bf16[16,4224]{1,0:T(8,128)(2,1)S(1)}, bf16[16,4224]{1,0:T(8,128)(2,1)S(1)}, u32[]{:S(2)}, u32[]{:S(2)}) collective-permute-start(bf16[16,4224]{1,0:T(8,128)(2,1)S(1)} %maximum_select_fusion.6), channel_id=1, source_target_pairs={{0,2},{1,3},{2,0},{3,1},{4,6},{5,7},{6,4},{7,5},{8,10},{9,11},{10,... | collective-permute-start | bytes 405512 | tf_op jit(solution)/shard_map/ppermute | solution.py:14
  7.3 6.7 %collective-permute-start.1 = (bf16[16,4096]{1,0:T(8,128)(2,1)S(1)}, bf16[16,4096]{1,0:T(8,128)(2,1)S(1)}, u32[]{:S(2)}, u32[]{:S(2)}) collective-permute-start(bf16[16,4096]{1,0:T(8,128)(2,1)S(1)} %maximum_select_fusion.7), channel_id=1, source_target_pairs={{0,2},{1,3},{2,0},{3,1},{4,6},{5,7},{6,4},{7,5},{8,10},{9,11},{10,... | collective-permute-start | bytes 393224 | tf_op jit(solution)/shard_map/ppermute | solution.py:14
  11.7 12.9 %collective-permute-start.6 = (bf16[32,4224]{1,0:T(8,128)(2,1)S(1)}, bf16[32,4224]{1,0:T(8,128)(2,1)S(1)}, u32[]{:S(2)}, u32[]{:S(2)}) collective-permute-start(bf16[32,4224]{1,0:T(8,128)(2,1)S(1)} %maximum_select_fusion.4), channel_id=1, source_target_pairs={{0,4},{1,5},{2,6},{3,7},{4,0},{5,1},{6,2},{7,3},{8,12},{9,13},{10,... | collective-permute-start | bytes 811016 | tf_op jit(solution)/shard_map/ppermute | solution.py:14
  14.1 47.5 %copy-start.3 = (bf16[1,8192,64]{1,2,0:T(8,128)(2,1)S(1)}, bf16[1,8192,64]{1,2,0:T(8,128)(2,1)}, u32[]{:S(2)}) copy-start(bf16[1,8192,64]{1,2,0:T(8,128)(2,1)} %param.10) | copy-start | bytes 3145732
  14.1 16.7 %collective-permute-start.2 = (bf16[32,4096]{1,0:T(8,128)(2,1)S(1)}, bf16[32,4096]{1,0:T(8,128)(2,1)S(1)}, u32[]{:S(2)}, u32[]{:S(2)}) collective-permute-start(bf16[32,4096]{1,0:T(8,128)(2,1)S(1)} %maximum_select_fusion.5), channel_id=1, source_target_pairs={{0,4},{1,5},{2,6},{3,7},{4,0},{5,1},{6,2},{7,3},{8,12},{9,13},{10,... | collective-permute-start | bytes 786440 | tf_op jit(solution)/shard_map/ppermute | solution.py:14
  24.7 36.5 %collective-permute-start.7 = (bf16[64,4224]{1,0:T(8,128)(2,1)S(1)}, bf16[64,4224]{1,0:T(8,128)(2,1)S(1)}, u32[]{:S(2)}, u32[]{:S(2)}) collective-permute-start(bf16[64,4224]{1,0:T(8,128)(2,1)S(1)} %maximum_select_fusion.2), channel_id=1, source_target_pairs={{0,8},{1,9},{2,10},{3,11},{4,12},{5,13},{6,14},{7,15},{8,0},{9,1},... | collective-permute-start | bytes 1622024 | tf_op jit(solution)/shard_map/ppermute | solution.py:14
  30.9 36.0 %collective-permute-start.3 = (bf16[64,4096]{1,0:T(8,128)(2,1)S(1)}, bf16[64,4096]{1,0:T(8,128)(2,1)S(1)}, u32[]{:S(2)}, u32[]{:S(2)}) collective-permute-start(bf16[64,4096]{1,0:T(8,128)(2,1)S(1)} %maximum_select_fusion.3), channel_id=1, source_target_pairs={{0,8},{1,9},{2,10},{3,11},{4,12},{5,13},{6,14},{7,15},{8,0},{9,1},... | collective-permute-start | bytes 1572872 | tf_op jit(solution)/shard_map/ppermute | solution.py:14
  95.6 6.6 %copy-start.2 = (bf16[16,64,1792]{2,1,0:T(8,128)(2,1)S(1)}, bf16[16,64,1792]{2,1,0:T(8,128)(2,1)}, u32[]{:S(2)}) copy-start(bf16[16,64,1792]{2,1,0:T(8,128)(2,1)} %param.11) | copy-start | bytes 11010052
  111.1 7.4 %copy-start.1 = (s32[16]{0:T(128)S(1)}, s32[16]{0:T(128)}, u32[]{:S(2)}) copy-start(s32[16]{0:T(128)} %param.13) | copy-start | bytes 196
